TPU v7x, 32 devices: a whole 2x2x4 slice. The times are simulated.
32 devices in a mesh: row: 8 (over y, x, core), col: 4 (over z).
Axes of the slice: x: 2, y: 2, z: 4, core: 2. Of those that a mesh axis runs over, the one named last changes fastest.
Arguments:
- tokens: bfloat16 [512, 8192], P('col', 'row'), may hold values from -6 to 6
- cotangent: bfloat16 [512, 8192], P('col', 'row'), may hold values from -1.5 to 1.5
- gate_weight: bfloat16 [8192, 28672], P('row', 'col'), may hold values from -0.0625 to 0.0625
- up_weight: bfloat16 [8192, 28672], P('row', 'col'), may hold values from -0.0625 to 0.0625
- down_weight: bfloat16 [28672, 8192], P('col', 'row'), may hold values from -0.03125 to 0.03125
Outputs:
- input_grad: bfloat16 [512, 8192], P('col', 'row')
- gate_grad: bfloat16 [8192, 28672], P('row', 'col')
- up_grad: bfloat16 [8192, 28672], P('row', 'col')
- down_grad: bfloat16 [28672, 8192], P('col', 'row')
All inputs are finite; a program needn't handle non-finite values.
Results may differ from a plain program's by a relative error of at most 0.02.
Values may be sent and summed in bfloat16 or wider, within the bound.
No kernel may reach another device: no remote copies, remote signals or barrier semaphores. Data moves between devices by JAX's collectives and lax.ppermute only.
A program may use at most 256 MiB of HBM per device.

v0:
```python
import jax
import jax.numpy as jnp
from jax import lax
from jax.sharding import PartitionSpec as P


def activations(sums, columns):
    gate = sums[:, :columns]
    up = sums[:, columns : 2 * columns]
    back = sums[:, 2 * columns :]
    sigma = jax.nn.sigmoid(gate)
    silu_gate = gate * sigma
    hidden = (silu_gate * up).astype(jnp.bfloat16)
    grad_gate_act = (back * up * sigma * (1.0 + gate * (1.0 - sigma))).astype(jnp.bfloat16)
    grad_up_act = (back * silu_gate).astype(jnp.bfloat16)
    return jnp.concatenate([hidden, grad_gate_act, grad_up_act], axis=1)


def contract_rows(left, right):
    return lax.dot_general(
        left, right, (((0,), (0,)), ((), ())), preferred_element_type=jnp.float32
    )


def contract_cols(left, right):
    return lax.dot_general(
        left, right, (((1,), (1,)), ((), ())), preferred_element_type=jnp.float32
    )


def per_device(tokens, cotangent, gate_weight, up_weight, down_weight):
    x_panel, dy_panel = (
        lax.all_gather(tokens, "col", axis=0, tiled=True),
        lax.all_gather(cotangent, "col", axis=0, tiled=True),
    )
    columns = gate_weight.shape[1]
    gate_part = jnp.dot(x_panel, gate_weight, preferred_element_type=jnp.float32)
    up_part = jnp.dot(x_panel, up_weight, preferred_element_type=jnp.float32)
    back_part = contract_cols(dy_panel, down_weight)
    sums = lax.psum_scatter(
        jnp.concatenate([gate_part, up_part, back_part], axis=1).astype(jnp.bfloat16),
        "row",
        scatter_dimension=0,
        tiled=True,
    ).astype(jnp.float32)
    packed = lax.all_gather(activations(sums, columns), "row", axis=0, tiled=True)
    hidden = packed[:, :columns]
    grad_gate_act = packed[:, columns : 2 * columns]
    grad_up_act = packed[:, 2 * columns :]
    down_grad = contract_rows(hidden, dy_panel).astype(jnp.bfloat16)
    gate_grad = contract_rows(x_panel, grad_gate_act).astype(jnp.bfloat16)
    up_grad = contract_rows(x_panel, grad_up_act).astype(jnp.bfloat16)
    input_sum = lax.psum_scatter(
        (contract_cols(grad_gate_act, gate_weight) + contract_cols(grad_up_act, up_weight)).astype(
            jnp.bfloat16
        ),
        "col",
        scatter_dimension=0,
        tiled=True,
    )
    return (input_sum, gate_grad, up_grad, down_grad)


def solution(mesh):
    in_specs = (P("col", "row"), P("col", "row"), P("row", "col"), P("row", "col"), P("col", "row"))
    out_specs = (P("col", "row"), P("row", "col"), P("row", "col"), P("col", "row"))
    return jax.shard_map(
        per_device, mesh=mesh, in_specs=in_specs, out_specs=out_specs, check_vma=False
    )
```

profile of v0, /device:TPU:0, one launch (start us, length us, event | category | flops | bytes accessed | tf_op | source)
XLA Modules:
  0.0 476.8 jit_solution(14434081499963626001)
XLA Ops:
  7.2 0.0 all-gather.4.cloned.1.call-start
  7.2 0.7 all-gather.4.cloned.1.call-update
  7.9 0.0 all-gather.6.cloned.1.call-start
  7.9 0.7 all-gather.6.cloned.1.call-update
  8.6 0.0 reduce-scatter.3.cloned.1.call-start
  8.7 31.5 %all-gather.4.cloned.1.call-done = bf16[512,1024]{1,0:T(8,128)(2,1)} async-done(((bf16[128,1024]{1,0:T(8,128)(2,1)}), bf16[512,1024]{1,0:T(8,128)(2,1)}) %all-gather.4.cloned.1.call-update) | async-done | bytes 1048592 | tf_op jit(solution)/shard_map/all_gather | solution.py:33
  40.2 0.0 copy-start
  40.2 15.1 %convolution_convert_fusion.2 = bf16[512,7168]{1,0:T(8,128)(2,1)} fusion(bf16[512,1024]{1,0:T(8,128)(2,1)} %all-gather.4.cloned.1.call-done, bf16[1024,7168]{1,0:T(8,128)(2,1)} %param.8), kind=kOutput, calls=%fused_computation.5 | convolution fusion | flops 7519862784 | bytes 23068672 | tf_op jit(solution)/shard_map/dot_general | solution.py:38
  55.3 0.0 copy-done
  55.3 15.0 %convolution_convert_fusion.3 = bf16[512,7168]{1,0:T(8,128)(2,1)} fusion(bf16[512,1024]{1,0:T(8,128)(2,1)S(1)} %copy-done, bf16[1024,7168]{1,0:T(8,128)(2,1)} %param.7), kind=kOutput, calls=%fused_computation.6 | convolution fusion | flops 7519862784 | bytes 23068672 | tf_op jit(solution)/shard_map/dot_general | solution.py:37
  70.3 0.0 all-gather.6.cloned.1.call-done
  70.4 13.2 %convolution_convert_fusion.1 = bf16[512,7168]{1,0:T(8,128)(2,1)} fusion(bf16[512,1024]{1,0:T(8,128)(2,1)} %all-gather.6.cloned.1.call-done, bf16[7168,1024]{1,0:T(8,128)(2,1)} %param.9), kind=kOutput, calls=%fused_computation.4 | convolution fusion | flops 7519862784 | bytes 23068672 | tf_op jit(solution)/shard_map/dot_general | solution.py:26
  83.5 19.6 %pad_maximum_fusion = bf16[512,21504]{1,0:T(8,128)(2,1)} fusion(bf16[512,7168]{1,0:T(8,128)(2,1)} %convolution_convert_fusion.1, bf16[512,7168]{1,0:T(8,128)(2,1)} %convolution_convert_fusion.2, bf16[512,7168]{1,0:T(8,128)(2,1)} %convolution_convert_fusion.3), kind=kLoop, calls=%fused_computation | loop fusion | flops 66060288 | bytes 44040192 | tf_op jit(solution)/shard_map/concatenate | solution.py:41
  103.1 0.0 reduce-scatter.3.cloned.1.call-update
  103.1 0.0 all-gather.8.cloned.1.call-start
  103.2 140.3 %reduce-scatter.3.cloned.1.call-done = bf16[64,21504]{1,0:T(8,128)(2,1)} async-done(((bf16[512,21504]{1,0:T(8,128)(2,1)}), bf16[64,21504]{1,0:T(8,128)(2,1)}) %reduce-scatter.3.cloned.1.call-update) | async-done | bytes 2752528 | tf_op jit(solution)/shard_map/reduce_scatter | solution.py:40
  243.5 2.1 convert_element_type.31
  245.6 1.1 multiply_convert_fusion.2
  246.7 1.7 pad_maximum_fusion.1
  248.4 0.0 all-gather.8.cloned.1.call-update
  248.4 0.2 reduce-scatter.5.cloned.1.call-start
  248.6 112.0 %all-gather.8.cloned.1.call-done = bf16[512,21504]{1,0:T(8,128)(2,1)} async-done(((bf16[64,21504]{1,0:T(8,128)(2,1)}), bf16[512,21504]{1,0:T(8,128)(2,1)}) %all-gather.8.cloned.1.call-update) | async-done | bytes 22020112 | tf_op jit(solution)/shard_map/all_gather | solution.py:46
  360.6 13.2 %fusion.2 = f32[512,1024]{1,0:T(8,128)S(1)} fusion(bf16[1024,7168]{1,0:T(8,128)(2,1)} %param.8, bf16[512,21504]{1,0:T(8,128)(2,1)} %all-gather.8.cloned.1.call-done), kind=kOutput, calls=%fused_computation.9 | convolution fusion | flops 7516192768 | bytes 24117248 | tf_op jit(solution)/shard_map/dot_general | solution.py:26
  373.7 14.0 %add_convert_fusion = bf16[512,1024]{1,0:T(8,128)(2,1)} fusion(f32[512,1024]{1,0:T(8,128)S(1)} %fusion.2, bf16[1024,7168]{1,0:T(8,128)(2,1)} %param.7, bf16[512,21504]{1,0:T(8,128)(2,1)} %all-gather.8.cloned.1.call-done), kind=kOutput, calls=%fused_computation.15 | convolution fusion | flops 7517241344 | bytes 25165824 | tf_op jit(solution)/shard_map/dot_general | solution.py:26
  387.8 0.0 reduce-scatter.5.cloned.1.call-update
  387.8 14.2 %convert_bitcast_fusion = bf16[1024,7168]{0,1:T(8,128)(2,1)} fusion(bf16[512,1024]{1,0:T(8,128)(2,1)S(1)} %copy-done, bf16[512,21504]{1,0:T(8,128)(2,1)} %all-gather.8.cloned.1.call-done), kind=kOutput, calls=%fused_computation.1 | convolution fusion | flops 7523532800 | bytes 23068672 | tf_op jit(solution)/shard_map/dot_general | solution.py:20
  402.0 19.9 %copy.10 = bf16[1024,7168]{1,0:T(8,128)(2,1)} copy(bf16[1024,7168]{0,1:T(8,128)(2,1)} %convert_bitcast_fusion) | data formatting | bytes 29360128
  421.9 14.2 %convert_bitcast_fusion.1 = bf16[1024,7168]{0,1:T(8,128)(2,1)} fusion(bf16[512,1024]{1,0:T(8,128)(2,1)S(1)} %copy-done, bf16[512,21504]{1,0:T(8,128)(2,1)} %all-gather.8.cloned.1.call-done), kind=kOutput, calls=%fused_computation.2 | convolution fusion | flops 7523532800 | bytes 23068672 | tf_op jit(solution)/shard_map/dot_general | solution.py:20
  436.1 0.0 copy-start.1
  436.1 20.0 %copy.9 = bf16[1024,7168]{1,0:T(8,128)(2,1)} copy(bf16[1024,7168]{0,1:T(8,128)(2,1)} %convert_bitcast_fusion.1) | data formatting | bytes 29360128
  456.1 0.0 copy-done.1
  456.1 14.2 %convolution_convert_fusion = bf16[7168,1024]{1,0:T(8,128)(2,1)} fusion(bf16[512,1024]{1,0:T(8,128)(2,1)S(1)} %copy-done.1, bf16[512,21504]{1,0:T(8,128)(2,1)} %all-gather.8.cloned.1.call-done), kind=kOutput, calls=%fused_computation.3 | convolution fusion | flops 7523532800 | bytes 23068672 | tf_op jit(solution)/shard_map/dot_general | solution.py:20
  (1 shorter events, 0.0 us)
Async XLA Ops:
  7.2 33.1 %all-gather.4.cloned.1.call-start = ((), (), s32[]{:S(2)}) async-start(), calls=%async_computation.2 | async-start | bytes 1310720 | tf_op jit(solution)/shard_map/all_gather | solution.py:33
  7.9 62.5 %all-gather.6.cloned.1.call-start = ((), (), s32[]{:S(2)}) async-start(), calls=%async_computation.3 | async-start | bytes 1310720 | tf_op jit(solution)/shard_map/all_gather | solution.py:34
  8.6 234.8 %reduce-scatter.3.cloned.1.call-start = ((), (), s32[]{:S(2)}) async-start(), calls=%async_computation.4 | async-start | bytes 24772608 | tf_op jit(solution)/shard_map/reduce_scatter | solution.py:40
  40.2 15.1 %copy-start = (bf16[512,1024]{1,0:T(8,128)(2,1)S(1)}, bf16[512,1024]{1,0:T(8,128)(2,1)}, u32[]{:S(2)}) copy-start(bf16[512,1024]{1,0:T(8,128)(2,1)} %all-gather.4.cloned.1.call-done) | copy-start | bytes 3145732
  103.1 257.4 %all-gather.8.cloned.1.call-start = ((), (), s32[]{:S(2)}) async-start(), calls=%async_computation.5 | async-start | bytes 24772608 | tf_op jit(solution)/shard_map/all_gather | solution.py:46
  248.4 221.9 %reduce-scatter.5.cloned.1.call-start = ((), (), s32[]{:S(2)}) async-start(), calls=%async_computation.6 | async-start | bytes 1310720 | tf_op jit(solution)/shard_map/reduce_scatter | solution.py:53
  436.1 20.0 %copy-start.1 = (bf16[512,1024]{1,0:T(8,128)(2,1)S(1)}, bf16[512,1024]{1,0:T(8,128)(2,1)}, u32[]{:S(2)}) copy-start(bf16[512,1024]{1,0:T(8,128)(2,1)} %all-gather.6.cloned.1.call-done) | copy-start | bytes 3145732
Sparse Core Ops, SparseCore 0:
  9.6 30.6 all-gather.3
  41.8 27.4 all-gather.5
  103.3 140.1 reduce-scatter.2
  248.5 112.0 all-gather.7
  387.9 27.1 reduce-scatter.4
where the time goes:
time: 478 us; the launch traced here: 477 us
  waiting for transfers between devices  285 us (60%)
  matrix products  113 us (24%)
  local copies, waits for them, and re-layouts  39.9 us (8%)
  other arithmetic  24.5 us (5%)
  between operations  13.8 us (3%)
    reduce_scatter x1, waiting for transfers between devices, per_device(): lax.psum_scatter(jnp.concatenate([gate_part, up_part, back_part], axis=1)...  140 us
    all_gather x1, waiting for transfers between devices, per_device(): lax.all_gather(activations(sums, columns), 'row', axis=0, tiled=True)  112 us
    dot_general x3, matrix products, contract_rows(): lax.dot_general(left, right, (((0,), (0,)), ((), ())), preferred_element_...  42.6 us
    dot_general x3, matrix products, contract_cols(): lax.dot_general(left, right, (((1,), (1,)), ((), ())), preferred_element_...  40.3 us
    unnamed x6, local copies, waits for them, and re-layouts  39.9 us
    all_gather x1, waiting for transfers between devices, per_device(): lax.all_gather(tokens, 'col', axis=0, tiled=True)  31.5 us
    concatenate x1, other arithmetic, per_device(): jnp.concatenate([gate_part, up_part, back_part], axis=1)  19.6 us
    dot_general x1, matrix products, per_device(): up_part = jnp.dot(x_panel, up_weight, preferred_element_type=jnp.float32)  15.1 us
  transfers between devices with their start and end apart: 5, of which 3 were waited for; matrix products, arithmetic and copies ran while one was open for 24% of the time, Pallas kernels for 0%

commit v1 on v0

--- a/solution.py
+++ b/solution.py
@@ -2,6 +2,23 @@
 import jax.numpy as jnp
 from jax import lax
 from jax.sharding import PartitionSpec as P
+
+
+def scan_the_orders(vector):
+    u1 = lax.axis_size("col")
+    then = lax.axis_index("col")
+    main, h_now, later = (u1, then, vector.shape[0])
+    sheets = tuple(((pp, (pp + 1) % main) for pp in range(main)))
+    heard = jnp.zeros((*vector.shape[:0], main * later, *vector.shape[1:]), vector.dtype)
+    big = vector
+    t = 0
+    while t < main:
+        clean = (h_now - t) % main
+        heard = lax.dynamic_update_slice_in_dim(heard, big, clean * later, axis=0)
+        if t < main - 1:
+            big = lax.ppermute(big, axis_name="col", perm=sheets)
+        t = t + 1
+    return heard
 
 
 def activations(sums, columns):
@@ -30,7 +47,7 @@
 
 def per_device(tokens, cotangent, gate_weight, up_weight, down_weight):
     x_panel, dy_panel = (
-        lax.all_gather(tokens, "col", axis=0, tiled=True),
+        scan_the_orders(tokens),
         lax.all_gather(cotangent, "col", axis=0, tiled=True),
     )
     columns = gate_weight.shape[1]

time: 478 us -> 433 us (0.906)
  local copies, waits for them, and re-layouts: 39.9 us -> 1.2 us
  matrix products: 113 us -> 108 us
    unnamed x6 -> x10, local copies, waits for them, and re-layouts: 39.9 us -> 0.03 us
    all_gather x1 -> x0, waiting for transfers between devices: 31.5 us -> none  [per_device(): lax.all_gather(tokens, 'col', axis=0, tiled=True)]
    ppermute x0 -> x3, waiting for transfers between devices: none -> 30.8 us  [scan_the_orders(): big = lax.ppermute(big, axis_name='col', perm=sheets)]
    dot_general x1, matrix products: 15 us -> 9.95 us  [per_device(): jnp.dot(x_panel, gate_weight, preferred_element_type=jnp.float32)]
  transfers between devices with their start and end apart: 5 -> 7, of which waited for: 3 -> 5; matrix products, arithmetic and copies ran while one was open for 24% -> 16% of each run, Pallas kernels for 0% -> 0%
where the time goes in v1:
time: 433 us
  waiting for transfers between devices  281 us (65%)
  matrix products  108 us (25%)
  other arithmetic  24.5 us (6%)
  between operations  14 us (3%)
    reduce_scatter x1, waiting for transfers between devices, per_device(): lax.psum_scatter(jnp.concatenate([gate_part, up_part, back_part], axis=1)...  138 us
    all_gather x1, waiting for transfers between devices, per_device(): lax.all_gather(activations(sums, columns), 'row', axis=0, tiled=True)  112 us
    dot_general x3, matrix products, contract_rows(): lax.dot_general(left, right, (((0,), (0,)), ((), ())), preferred_element_...  42.7 us
    dot_general x3, matrix products, contract_cols(): lax.dot_general(left, right, (((1,), (1,)), ((), ())), preferred_element_...  40.4 us
    ppermute x3, waiting for transfers between devices, scan_the_orders(): big = lax.ppermute(big, axis_name='col', perm=sheets)  30.8 us
    concatenate x1, other arithmetic, per_device(): jnp.concatenate([gate_part, up_part, back_part], axis=1)  19.6 us
    dot_general x1, matrix products, per_device(): up_part = jnp.dot(x_panel, up_weight, preferred_element_type=jnp.float32)  15.2 us
    dot_general x1, matrix products, per_device(): jnp.dot(x_panel, gate_weight, preferred_element_type=jnp.float32)  9.95 us
  transfers between devices with their start and end apart: 7, of which 5 were waited for; matrix products, arithmetic and copies ran while one was open for 16% of the time, Pallas kernels for 0%

profile of v1, /device:TPU:0, one launch (start us, length us, event | category | flops | bytes accessed | tf_op | source)
XLA Modules:
  0.0 432.5 jit_solution(14688852444827249374)
XLA Ops:
  7.2 0.0 all-gather.3.cloned.1.call-start
  7.2 3.1 collective-permute-start
  10.3 8.5 %collective-permute-done = bf16[128,1024]{1,0:T(8,128)(2,1)S(1)} collective-permute-done((bf16[128,1024]{1,0:T(8,128)(2,1)}, bf16[128,1024]{1,0:T(8,128)(2,1)S(1)}, u32[]{:S(2)}, u32[]{:S(2)}) %collective-permute-start) | collective-permute-done | bytes 262176 | tf_op jit(solution)/shard_map/ppermute | solution.py:19
  18.8 0.0 collective-permute-start.1
  18.8 0.0 all-gather.3.cloned.1.call-update
  18.9 0.0 reduce-scatter.3.cloned.1.call-start
  18.9 9.2 %collective-permute-done.1 = bf16[128,1024]{1,0:T(8,128)(2,1)S(1)} collective-permute-done((bf16[128,1024]{1,0:T(8,128)(2,1)S(1)}, bf16[128,1024]{1,0:T(8,128)(2,1)S(1)}, u32[]{:S(2)}, u32[]{:S(2)}) %collective-permute-start.1) | collective-permute-done | bytes 262176 | tf_op jit(solution)/shard_map/ppermute | solution.py:19
  28.1 0.0 collective-permute-start.2
  28.1 0.1 broadcast_in_dim.3
  28.2 1.0 constant_dynamic-update-slice_fusion.3
  29.4 13.0 %collective-permute-done.2 = bf16[128,1024]{1,0:T(8,128)(2,1)S(1)} collective-permute-done((bf16[128,1024]{1,0:T(8,128)(2,1)S(1)}, bf16[128,1024]{1,0:T(8,128)(2,1)S(1)}, u32[]{:S(2)}, u32[]{:S(2)}) %collective-permute-start.2) | collective-permute-done | bytes 262176 | tf_op jit(solution)/shard_map/ppermute | solution.py:19
  42.4 0.0 slice-start.1
  42.4 0.0 slice-start.2
  42.5 15.2 %convolution_convert_fusion.4 = bf16[512,7168]{1,0:T(8,128)(2,1)} fusion(bf16[512,1024]{1,0:T(8,128)(2,1)S(1)} %constant_dynamic-update-slice_fusion, bf16[1024,7168]{1,0:T(8,128)(2,1)} %param.8), kind=kOutput, calls=%fused_computation.5 | convolution fusion | flops 7519862784 | bytes 23068672 | tf_op jit(solution)/shard_map/dot_general | solution.py:55
  57.7 9.9 %convolution_convert_fusion.5 = bf16[512,7168]{1,0:T(8,128)(2,1)} fusion(bf16[512,1024]{1,0:T(8,128)(2,1)S(1)} %constant_dynamic-update-slice_fusion, bf16[1024,7168]{1,0:T(8,128)(2,1)S(1)} %bitcast.12), kind=kOutput, calls=%fused_computation.6 | convolution fusion | flops 7519862784 | bytes 23068672 | tf_op jit(solution)/shard_map/dot_general | solution.py:54
  67.6 13.2 %convolution_convert_fusion.3 = bf16[512,7168]{1,0:T(8,128)(2,1)} fusion(bf16[512,1024]{1,0:T(8,128)(2,1)} %all-gather.3.cloned.1.call-done, bf16[7168,1024]{1,0:T(8,128)(2,1)} %param.9), kind=kOutput, calls=%fused_computation.4 | convolution fusion | flops 7519862784 | bytes 23068672 | tf_op jit(solution)/shard_map/dot_general | solution.py:43
  80.8 19.6 %pad_maximum_fusion = bf16[512,21504]{1,0:T(8,128)(2,1)} fusion(bf16[512,7168]{1,0:T(8,128)(2,1)} %convolution_convert_fusion.3, bf16[512,7168]{1,0:T(8,128)(2,1)} %convolution_convert_fusion.4, bf16[512,7168]{1,0:T(8,128)(2,1)} %convolution_convert_fusion.5), kind=kLoop, calls=%fused_computation | loop fusion | flops 66060288 | bytes 44040192 | tf_op jit(solution)/shard_map/concatenate | solution.py:58
  100.4 0.0 reduce-scatter.3.cloned.1.call-update
  100.4 0.2 all-gather.5.cloned.1.call-start
  100.6 138.2 %reduce-scatter.3.cloned.1.call-done = bf16[64,21504]{1,0:T(8,128)(2,1)} async-done(((bf16[512,21504]{1,0:T(8,128)(2,1)}), bf16[64,21504]{1,0:T(8,128)(2,1)}) %reduce-scatter.3.cloned.1.call-update) | async-done | bytes 2752528 | tf_op jit(solution)/shard_map/reduce_scatter | solution.py:57
  238.9 2.1 convert_element_type.25
  241.0 1.1 multiply_convert_fusion.2
  242.1 1.7 pad_maximum_fusion.1
  243.8 0.0 all-gather.5.cloned.1.call-update
  243.8 0.0 reduce-scatter.5.cloned.1.call-start
  243.9 112.1 %all-gather.5.cloned.1.call-done = bf16[512,21504]{1,0:T(8,128)(2,1)} async-done(((bf16[64,21504]{1,0:T(8,128)(2,1)}), bf16[512,21504]{1,0:T(8,128)(2,1)}) %all-gather.5.cloned.1.call-update) | async-done | bytes 22020112 | tf_op jit(solution)/shard_map/all_gather | solution.py:63
  356.0 13.2 %fusion.2 = f32[512,1024]{1,0:T(8,128)S(1)} fusion(bf16[1024,7168]{1,0:T(8,128)(2,1)} %param.8, bf16[512,21504]{1,0:T(8,128)(2,1)} %all-gather.5.cloned.1.call-done), kind=kOutput, calls=%fused_computation.9 | convolution fusion | flops 7516192768 | bytes 24117248 | tf_op jit(solution)/shard_map/dot_general | solution.py:43
  369.1 14.1 %add_convert_fusion = bf16[512,1024]{1,0:T(8,128)(2,1)} fusion(f32[512,1024]{1,0:T(8,128)S(1)} %fusion.2, bf16[1024,7168]{1,0:T(8,128)(2,1)} %param.7, bf16[512,21504]{1,0:T(8,128)(2,1)} %all-gather.5.cloned.1.call-done), kind=kOutput, calls=%fused_computation.15 | convolution fusion | flops 7517241344 | bytes 25165824 | tf_op jit(solution)/shard_map/dot_general | solution.py:43
  383.2 0.0 reduce-scatter.5.cloned.1.call-update
  383.3 14.3 %convolution_convert_fusion.2 = bf16[1024,7168]{1,0:T(8,128)(2,1)} fusion(bf16[512,1024]{1,0:T(8,128)(2,1)S(1)} %constant_dynamic-update-slice_fusion, bf16[512,21504]{1,0:T(8,128)(2,1)} %all-gather.5.cloned.1.call-done), kind=kOutput, calls=%fused_computation.3 | convolution fusion | flops 7523532800 | bytes 23068672 | tf_op jit(solution)/shard_map/dot_general | solution.py:37
  397.6 14.2 %convolution_convert_fusion = bf16[7168,1024]{1,0:T(8,128)(2,1)} fusion(bf16[512,1024]{1,0:T(8,128)(2,1)S(1)} %copy-done, bf16[512,21504]{1,0:T(8,128)(2,1)} %all-gather.5.cloned.1.call-done), kind=kOutput, calls=%fused_computation.1 | convolution fusion | flops 7523532800 | bytes 23068672 | tf_op jit(solution)/shard_map/dot_general | solution.py:37
  411.8 14.2 %convolution_convert_fusion.1 = bf16[1024,7168]{1,0:T(8,128)(2,1)} fusion(bf16[512,1024]{1,0:T(8,128)(2,1)S(1)} %constant_dynamic-update-slice_fusion, bf16[512,21504]{1,0:T(8,128)(2,1)} %all-gather.5.cloned.1.call-done), kind=kOutput, calls=%fused_computation.2 | convolution fusion | flops 7523532800 | bytes 23068672 | tf_op jit(solution)/shard_map/dot_general | solution.py:37
  (14 shorter events, 0.1 us)
Async XLA Ops:
  7.2 60.5 %all-gather.3.cloned.1.call-start = ((), (), s32[]{:S(2)}) async-start(), calls=%async_computation.2 | async-start | bytes 1310720 | tf_op jit(solution)/shard_map/all_gather | solution.py:51
  7.2 11.6 %collective-permute-start = (bf16[128,1024]{1,0:T(8,128)(2,1)}, bf16[128,1024]{1,0:T(8,128)(2,1)S(1)}, u32[]{:S(2)}, u32[]{:S(2)}) collective-permute-start(bf16[128,1024]{1,0:T(8,128)(2,1)} %param.5), channel_id=1, source_target_pairs={{0,1},{1,2},{2,3},{3,0},{4,5},{5,6},{6,7},{7,4},{8,9},{9,10},{10,1... | collective-permute-start | bytes 786440 | tf_op jit(solution)/shard_map/ppermute | solution.py:19
  18.8 9.3 %collective-permute-start.1 = (bf16[128,1024]{1,0:T(8,128)(2,1)S(1)}, bf16[128,1024]{1,0:T(8,128)(2,1)S(1)}, u32[]{:S(2)}, u32[]{:S(2)}) collective-permute-start(bf16[128,1024]{1,0:T(8,128)(2,1)S(1)} %collective-permute-done), channel_id=1, source_target_pairs={{0,1},{1,2},{2,3},{3,0},{4,5},{5,6},{6,7},{7,4},{8,9},{9,10},{10,1... | collective-permute-start | bytes 786440 | tf_op jit(solution)/shard_map/ppermute | solution.py:19
  18.9 220.0 %reduce-scatter.3.cloned.1.call-start = ((), (), s32[]{:S(2)}) async-start(), calls=%async_computation.3 | async-start | bytes 24772608 | tf_op jit(solution)/shard_map/reduce_scatter | solution.py:57
  28.1 14.3 %collective-permute-start.2 = (bf16[128,1024]{1,0:T(8,128)(2,1)S(1)}, bf16[128,1024]{1,0:T(8,128)(2,1)S(1)}, u32[]{:S(2)}, u32[]{:S(2)}) collective-permute-start(bf16[128,1024]{1,0:T(8,128)(2,1)S(1)} %collective-permute-done.1), channel_id=1, source_target_pairs={{0,1},{1,2},{2,3},{3,0},{4,5},{5,6},{6,7},{7,4},{8,9},{9,10},{10,1... | collective-permute-start | bytes 786440 | tf_op jit(solution)/shard_map/ppermute | solution.py:19
  42.4 15.2 %slice-start = ((s8[14680064]{0:T(1024)(128)(4,1)}), s8[4194304]{0:T(1024)(128)(4,1)S(1)}, s32[]{:S(2)}) async-start(s8[14680064]{0:T(1024)(128)(4,1)} %bitcast.11), calls=%async_computation.6 | async-start | bytes 8388608
  42.4 15.2 %slice-start.1 = ((s8[14680064]{0:T(1024)(128)(4,1)}), s8[4194304]{0:T(1024)(128)(4,1)S(1)}, s32[]{:S(2)}) async-start(s8[14680064]{0:T(1024)(128)(4,1)} %bitcast.11), calls=%async_computation.7 | async-start | bytes 8388608
  42.4 15.2 %slice-start.2 = ((s8[14680064]{0:T(1024)(128)(4,1)}), s8[4194304]{0:T(1024)(128)(4,1)S(1)}, s32[]{:S(2)}) async-start(s8[14680064]{0:T(1024)(128)(4,1)} %bitcast.11), calls=%async_computation.8 | async-start | bytes 8388608
  42.5 15.2 %slice-start.3 = ((s8[14680064]{0:T(1024)(128)(4,1)}), s8[2097152]{0:T(1024)(128)(4,1)S(1)}, s32[]{:S(2)}) async-start(s8[14680064]{0:T(1024)(128)(4,1)} %bitcast.11), calls=%async_computation.9 | async-start | bytes 4194304
  100.4 255.6 %all-gather.5.cloned.1.call-start = ((), (), s32[]{:S(2)}) async-start(), calls=%async_computation.4 | async-start | bytes 24772608 | tf_op jit(solution)/shard_map/all_gather | solution.py:63
  243.8 182.2 %reduce-scatter.5.cloned.1.call-start = ((), (), s32[]{:S(2)}) async-start(), calls=%async_computation.5 | async-start | bytes 1310720 | tf_op jit(solution)/shard_map/reduce_scatter | solution.py:70
  383.3 14.3 %copy-start = (bf16[512,1024]{1,0:T(8,128)(2,1)S(1)}, bf16[512,1024]{1,0:T(8,128)(2,1)}, u32[]{:S(2)}) copy-start(bf16[512,1024]{1,0:T(8,128)(2,1)} %all-gather.3.cloned.1.call-done) | copy-start | bytes 3145732
Sparse Core Ops, SparseCore 0:
  19.0 34.7 all-gather.2
  100.5 138.2 reduce-scatter.2
  243.9 111.9 all-gather.4
  383.4 27.1 reduce-scatter.4
